TPU v7x, 32 devices: a whole 2x2x4 slice. The times are simulated.
32 devices in a mesh: shard: 4 (over z), rep: 8 (over y, x, core).
Axes of the slice: x: 2, y: 2, z: 4, core: 2. Of those that a mesh axis runs over, the one named last changes fastest.
Arguments:
- grads: bfloat16 [1, 8192, 28672], P(None, 'shard', 'rep'), may hold values from -81 to 81
- seeds: int32 [1], replicated, may hold values from 0 to 999999
Outputs:
- projected: bfloat16 [512, 1, 28672], P('shard', None, 'rep')
All inputs are finite; a program needn't handle non-finite values.
Results may differ from a plain program's by a relative error of at most 0.0056.
Values may be sent and summed in bfloat16 or wider, within the bound.
No kernel may reach another device: no remote copies, remote signals or barrier semaphores. Data moves between devices by JAX's collectives and lax.ppermute only.
A program may use at most 128 MiB of HBM per device.

v0:
```python
import jax
import jax.numpy as jnp
from jax import lax
from jax.sharding import PartitionSpec as P

RANK = 512
mix_first = 668265263
mix_second = -2048144789
mix_third = -1028477387


def sketch_table(seeds, first_row, count, rank):
    rows = first_row + lax.iota(jnp.int32, count)
    columns = lax.iota(jnp.int32, rank)
    counter = rows[:, None] * jnp.int32(rank) + columns[None, :]
    hashed = jnp.bitwise_xor(counter[None, :, :], (seeds * jnp.int32(mix_first))[:, None, None])
    hashed = hashed * jnp.int32(mix_second)
    hashed = jnp.bitwise_xor(hashed, lax.shift_right_logical(hashed, jnp.int32(15)))
    hashed = hashed * jnp.int32(mix_third)
    hashed = jnp.bitwise_xor(hashed, lax.shift_right_logical(hashed, jnp.int32(13)))
    unit = lax.shift_right_logical(hashed, jnp.int32(8)).astype(jnp.float32) * (1.0 / 16777216.0)
    return (2.0 * unit - 1.0).astype(jnp.bfloat16)


def body(grads, seeds):
    mats, depth, width = grads.shape
    rows_whole = lax.all_to_all(grads, "rep", split_axis=1, concat_axis=2, tiled=True)
    block = rows_whole.shape[2] // 8

    def add_block(step, total):
        start = step * block
        table = sketch_table(seeds, start, block, RANK)
        piece = lax.dynamic_slice_in_dim(rows_whole, start, block, 2)
        return total + jnp.einsum("mdc,mcr->dmr", piece, table, preferred_element_type=jnp.float32)

    sketch_rows = lax.fori_loop(
        0, 8, add_block, jnp.zeros((rows_whole.shape[1], mats, RANK), jnp.float32)
    )
    local_gram = jnp.einsum(
        "dmr,dms->mrs",
        sketch_rows,
        sketch_rows,
        precision=lax.Precision.HIGHEST,
        preferred_element_type=jnp.float32,
    )
    gram = lax.psum(local_gram, ("shard", "rep"))
    factor = jnp.linalg.cholesky(gram)
    own_rows = jnp.transpose(sketch_rows, (1, 0, 2))
    basis_rows = lax.linalg.triangular_solve(
        factor, own_rows, left_side=False, lower=True, transpose_a=True
    ).astype(jnp.bfloat16)
    partial_sum = jnp.einsum(
        "mdr,mdc->rmc",
        lax.all_gather(basis_rows, "rep", axis=1, tiled=True),
        grads,
        preferred_element_type=jnp.float32,
    )
    projected = lax.psum_scatter(partial_sum, "shard", scatter_dimension=0, tiled=True)
    return projected.astype(jnp.bfloat16)


def solution(mesh):
    return jax.shard_map(
        body,
        mesh=mesh,
        in_specs=(P(None, "shard", "rep"), P()),
        out_specs=P("shard", None, "rep"),
        check_vma=False,
    )
```

profile of v0, /device:TPU:0, one launch (start us, length us, event | category | flops | bytes accessed | tf_op | source)
XLA Modules:
  0.0 861.6 jit_solution(14677463218900408071)
XLA Ops:
  6.5 26.0 %copy.30 = bf16[1,2048,3584]{2,0,1:T(2,128)(2,1)} copy(bf16[1,2048,3584]{2,1,0:T(8,128)(2,1)} %param.4) | data formatting | bytes 29360128 | tf_op args[0]
  33.1 94.1 %reduce.36 = bf16[2048,3584]{1,0:T(8,128)(2,1)} reduce(bf16[2048,1,3584]{2,1,0:T(2,128)(2,1)} %bitcast.210, bf16[]{:T(256)} %broadcast.502), dimensions={1}, to_apply=%bitcast.195.reduce_sub_computation | reduce | bytes 29360130
  127.2 16.3 %reshape.459 = bf16[8,2,458752]{2,1,0:T(2,128)(2,1)} reshape(bf16[2048,3584]{1,0:T(8,128)(2,1)} %reduce.36) | data formatting | bytes 29360128
  143.5 5.6 all-to-all-start
  149.9 161.3 %all-to-all-done = bf16[8,2,458752]{2,1,0:T(2,128)(2,1)} async-done(((bf16[8,2,458752]{2,1,0:T(2,128)(2,1)}), bf16[8,2,458752]{2,1,0:T(2,128)(2,1)}, u32[]{:S(2)}, u32[]{:S(2)}) %all-to-all-start) | async-done | bytes 14680096 | tf_op jit(solution)/shard_map/all_to_all | solution.py:27
  311.2 20.2 %reshape.460 = bf16[2048,1,3584]{2,1,0:T(2,128)(2,1)} reshape(bf16[8,2,458752]{2,1,0:T(2,128)(2,1)} %all-to-all-done) | data formatting | bytes 29360128
  331.4 19.4 %copy.28 = bf16[1,2048,3584]{2,1,0:T(8,128)(2,1)} copy(bf16[1,2048,3584]{2,0,1:T(2,128)(2,1)} %bitcast.211) | data formatting | bytes 29360128
  350.8 18.7 %copy.21 = bf16[1,256,8,3584]{1,3,2,0:T(8,128)(2,1)} copy(bf16[1,256,8,3584]{3,1,2,0:T(8,128)(2,1)} %bitcast.212) | data formatting | bytes 29360128 | tf_op jit(solution)/shard_map/all_to_all | solution.py:27
  369.5 42.8 %while.18 = (s32[]{:T(128)}, f32[256,1,512]{0,2,1:T(8,128)S(1)}, s32[1]{0:T(128)}, bf16[1,256,28672]{1,2,0:T(8,128)(2,1)}, s32[]{:T(128)}, /*index=5*/s32[]{:T(128)}, s32[]{:T(128)}, s32[]{:T(128)}) while((s32[]{:T(128)}, f32[256,1,512]{0,2,1:T(8,128)S(1)}, s32[1]{0:T(128)}, bf16[1,256,28672]{1,2,0:T(8,128)(2,1)}, s32[]{:T(128)}, ...), condition=%wide.region_1.0_spmd.clone, body=%wide.region_0.0_spmd.clone.sunk | while | flops 963648512 | bytes 2912917 | solution.py:36
  380.2 5.3 fusion.77
  390.9 5.3 fusion.77
  414.9 130.6 %all-reduce.3.cloned.1.call-done = f32[1,512,512]{1,2,0:T(8,128)} async-done(((f32[1,512,512]{1,2,0:T(8,128)}), f32[1,512,512]{1,2,0:T(8,128)}) %all-reduce.3.cloned.1.call-update) | async-done | bytes 1048592 | tf_op jit(solution)/shard_map/psum | solution.py:46
  548.5 11.7 %custom-call.34 = f32[1,128,128]{2,1,0:T(8,128)S(1)} custom-call(f32[1,128,128]{2,1,0:T(8,128)S(1)} %cholesky.267), custom_call_target="Cholesky" | custom-call | tf_op jit(solution)/shard_map/jit(cholesky)/cholesky | solution.py:47
  560.3 9.8 %custom-call.35 = f32[1,1,128,128]{2,3,1,0:T(8,128)S(1)} custom-call(f32[1,1,128,128]{3,2,1,0:T(8,128)S(1)} %get-tuple-element.173), custom_call_target="InvertDiagBlocksLowerTriangular" | custom-call | tf_op jit(solution)/shard_map/jit(cholesky)/cholesky | solution.py:47
  570.9 11.7 %custom-call.36 = f32[1,128,128]{2,1,0:T(8,128)S(1)} custom-call(f32[1,128,128]{2,1,0:T(8,128)S(1)} %cholesky.271), custom_call_target="Cholesky" | custom-call | tf_op jit(solution)/shard_map/jit(cholesky)/cholesky | solution.py:47
  582.6 10.2 %custom-call.37 = f32[1,1,128,128]{2,3,1,0:T(8,128)S(1)} custom-call(f32[1,1,128,128]{3,2,1,0:T(8,128)S(1)} %get-tuple-element.170), custom_call_target="InvertDiagBlocksLowerTriangular" | custom-call | tf_op jit(solution)/shard_map/jit(cholesky)/cholesky | solution.py:47
  593.5 11.7 %custom-call.38 = f32[1,128,128]{2,1,0:T(8,128)S(1)} custom-call(f32[1,128,128]{2,1,0:T(8,128)S(1)} %cholesky.276), custom_call_target="Cholesky" | custom-call | tf_op jit(solution)/shard_map/jit(cholesky)/cholesky | solution.py:47
  606.0 9.8 %custom-call.39 = f32[1,1,128,128]{2,3,1,0:T(8,128)S(1)} custom-call(f32[1,1,128,128]{3,2,1,0:T(8,128)S(1)} %get-tuple-element.167), custom_call_target="InvertDiagBlocksLowerTriangular" | custom-call | tf_op jit(solution)/shard_map/jit(cholesky)/cholesky | solution.py:47
  616.4 11.7 %custom-call.40 = f32[1,128,128]{2,1,0:T(8,128)S(1)} custom-call(f32[1,128,128]{2,1,0:T(8,128)S(1)} %fusion.46), custom_call_target="Cholesky" | custom-call | tf_op jit(solution)/shard_map/jit(cholesky)/cholesky | solution.py:47
  632.3 8.1 while.17
  640.4 39.3 %custom-call.41 = f32[1,4,128,128]{2,3,1,0:T(8,128)S(1)} custom-call(f32[1,4,128,128]{3,2,1,0:T(8,128)S(1)} %bitcast.221), custom_call_target="InvertDiagBlocksLowerTriangular" | custom-call | tf_op jit(solution)/shard_map/triangular_solve | solution.py:49
  683.7 27.2 %all-gather.2.cloned.1.call-done = bf16[1,2048,512]{1,2,0:T(8,128)(2,1)} async-done(((bf16[1,256,512]{1,2,0:T(8,128)(2,1)}), bf16[1,2048,512]{1,2,0:T(8,128)(2,1)}) %all-gather.2.cloned.1.call-update) | async-done | bytes 2097168 | tf_op jit(solution)/shard_map/all_gather | solution.py:54
  710.9 13.5 %fusion.31 = f32[512,1,3584]{2,0,1:T(8,128)} fusion(bf16[1,2048,3584]{2,1,0:T(8,128)(2,1)} %param.4, bf16[1,2048,512]{1,2,0:T(8,128)(2,1)} %all-gather.2.cloned.1.call-done), kind=kOutput, calls=%fused_computation.27 | convolution fusion | flops 7516192768 | bytes 24117248 | tf_op jit(solution)/shard_map/mdr,mdc->rmc/dot_general | solution.py:52
  724.4 127.9 %reduce-scatter.2.cloned.1.call-done = f32[128,1,3584]{2,0,1:T(8,128)} async-done(((f32[512,1,3584]{2,0,1:T(8,128)}), f32[128,1,3584]{2,0,1:T(8,128)}) %reduce-scatter.2.cloned.1.call-update) | async-done | bytes 1835024 | tf_op jit(solution)/shard_map/reduce_scatter | solution.py:58
  (68 shorter events, 57.1 us)
Async XLA Ops:
  143.5 167.7 %all-to-all-start = ((bf16[8,2,458752]{2,1,0:T(2,128)(2,1)}), bf16[8,2,458752]{2,1,0:T(2,128)(2,1)}, u32[]{:S(2)}, u32[]{:S(2)}) async-start(bf16[8,2,458752]{2,1,0:T(2,128)(2,1)} %reshape.459), calls=%async_computation | async-start | bytes 29360128 | tf_op jit(solution)/shard_map/all_to_all | solution.py:27
  149.1 396.4 %all-reduce.3.cloned.1.call-start = ((), (), s32[]{:S(2)}) async-start(), calls=%async_computation.2 | async-start | bytes 2097152 | tf_op jit(solution)/shard_map/psum | solution.py:46
  414.4 296.5 %all-gather.2.cloned.1.call-start = ((), (), s32[]{:S(2)}) async-start(), calls=%async_computation.3 | async-start | bytes 2359296 | tf_op jit(solution)/shard_map/all_gather | solution.py:54
  683.6 168.7 %reduce-scatter.2.cloned.1.call-start = ((), (), s32[]{:S(2)}) async-start(), calls=%async_computation.4 | async-start | bytes 9175040 | tf_op jit(solution)/shard_map/reduce_scatter | solution.py:58
Sparse Core Ops, SparseCore 0:
  414.5 130.9 all-reduce.2
  683.8 27.0 all-gather.1
  724.5 127.7 reduce-scatter.1
where the time goes:
time: 869 us; the launch traced here: 862 us
  waiting for transfers between devices  447 us (51%)
  other arithmetic  217 us (25%)
  local copies, waits for them, and re-layouts  111 us (13%)
  matrix products  63 us (7%)
  between operations  16.7 us (2%)
    all_to_all x1, waiting for transfers between devices, body(): lax.all_to_all(grads, 'rep', split_axis=1, concat_axis=2, tiled=True)  161 us
    psum x1, waiting for transfers between devices, body(): gram = lax.psum(local_gram, ('shard', 'rep'))  131 us
    reduce_scatter x1, waiting for transfers between devices, body(): lax.psum_scatter(partial_sum, 'shard', scatter_dimension=0, tiled=True)  128 us
    unnamed x3, other arithmetic  94.1 us
    unnamed x5, local copies, waits for them, and re-layouts  82.4 us
    another operation x14, other arithmetic, body(): factor = jnp.linalg.cholesky(gram)  79 us
    dot_general x8, matrix products, add_block(): jnp.einsum('mdc,mcr->dmr', piece, table, preferred_element_type=jnp.float32)  42.5 us
    another operation x4, other arithmetic, body(): lax.linalg.triangular_solve(factor, own_rows, left_side=False, lower=True...  40.2 us
  transfers between devices with their start and end apart: 4, of which 4 were waited for; matrix products, arithmetic and copies ran while one was open for 0% of the time, Pallas kernels for 0%

commit v1 on v0

--- a/solution.py
+++ b/solution.py
@@ -24,7 +24,10 @@
 
 def body(grads, seeds):
     mats, depth, width = grads.shape
-    rows_whole = lax.all_to_all(grads, "rep", split_axis=1, concat_axis=2, tiled=True)
+    rows_whole = jnp.concatenate(
+        lax.all_to_all(jnp.stack(jnp.split(grads, lax.axis_size("rep"), axis=1)), "rep", 0, 0),
+        axis=2,
+    )
     block = rows_whole.shape[2] // 8
 
     def add_block(step, total):

time: 869 us -> 709 us (0.82)
  other arithmetic: 217 us -> 123 us
  local copies, waits for them, and re-layouts: 111 us -> 46.6 us
    unnamed x3 -> x2, other arithmetic: 94.1 us -> 0.01 us
    unnamed x5 -> x7, local copies, waits for them, and re-layouts: 82.4 us -> 20.2 us
    all_to_all x1 -> x0, local copies, waits for them, and re-layouts: 18.7 us -> none  [body(): lax.all_to_all(grads, 'rep', split_axis=1, concat_axis=2, tiled=True)]
    reshape x0 -> x1, local copies, waits for them, and re-layouts: none -> 13.7 us  [body(): jnp.concatenate(lax.all_to_all(jnp.stack(jnp.split(grads, lax.axis_size('...]
where the time goes in v1:
time: 709 us; the launch traced here: 703 us
  waiting for transfers between devices  447 us (63%)
  other arithmetic  123 us (17%)
  matrix products  63.1 us (9%)
  local copies, waits for them, and re-layouts  46.6 us (7%)
  between operations  16.8 us (2%)
    all_to_all x1, waiting for transfers between devices, body(): lax.all_to_all(jnp.stack(jnp.split(grads, lax.axis_size('rep'), axis=1)),...  161 us
    psum x1, waiting for transfers between devices, body(): gram = lax.psum(local_gram, ('shard', 'rep'))  130 us
    reduce_scatter x1, waiting for transfers between devices, body(): lax.psum_scatter(partial_sum, 'shard', scatter_dimension=0, tiled=True)  128 us
    another operation x14, other arithmetic, body(): factor = jnp.linalg.cholesky(gram)  78.8 us
    dot_general x8, matrix products, add_block(): jnp.einsum('mdc,mcr->dmr', piece, table, preferred_element_type=jnp.float32)  42.5 us
    another operation x4, other arithmetic, body(): lax.linalg.triangular_solve(factor, own_rows, left_side=False, lower=True...  40.2 us
    all_gather x1, waiting for transfers between devices, body(): lax.all_gather(basis_rows, 'rep', axis=1, tiled=True)  27.2 us
    unnamed x7, local copies, waits for them, and re-layouts  20.2 us
  transfers between devices with their start and end apart: 4, of which 4 were waited for; matrix products, arithmetic and copies ran while one was open for 0% of the time, Pallas kernels for 0%

profile of v1, /device:TPU:0, one launch (start us, length us, event | category | flops | bytes accessed | tf_op | source)
XLA Modules:
  0.0 702.9 jit_solution(16570029235851708633)
XLA Ops:
  29.6 5.5 all-to-all-start
  35.8 161.4 %all-to-all-done = bf16[8,1,256,3584]{3,2,1,0:T(8,128)(2,1)} async-done(((bf16[8,1,256,3584]{3,2,1,0:T(8,128)(2,1)}), bf16[8,1,256,3584]{3,2,1,0:T(8,128)(2,1)}, u32[]{:S(2)}, u32[]{:S(2)}) %all-to-all-start) | async-done | bytes 14680096 | tf_op jit(solution)/shard_map/all_to_all | solution.py:28
  197.3 13.7 %copy.12 = bf16[8,1,32,8,3584]{4,3,0,2,1:T(8,128)(2,1)} copy(bf16[8,1,32,8,3584]{4,3,2,1,0:T(8,128)(2,1)} %bitcast.69) | data formatting | bytes 29360128 | tf_op jit(solution)/shard_map/reshape | solution.py:27
  210.9 42.8 %while.18 = (s32[]{:T(128)}, f32[256,1,512]{0,2,1:T(8,128)S(1)}, s32[1]{0:T(128)}, bf16[1,256,28672]{2,1,0:T(8,128)(2,1)}, s32[]{:T(128)}, /*index=5*/s32[]{:T(128)}, s32[]{:T(128)}, s32[]{:T(128)}) while((s32[]{:T(128)}, f32[256,1,512]{0,2,1:T(8,128)S(1)}, s32[1]{0:T(128)}, bf16[1,256,28672]{2,1,0:T(8,128)(2,1)}, s32[]{:T(128)}, ...), condition=%wide.region_1.0_spmd.clone, body=%wide.region_0.0_spmd.clone.sunk | while | flops 963648512 | bytes 2912917 | solution.py:39
  216.3 5.3 fusion.77
  221.6 5.3 fusion.77
  227.0 5.3 fusion.77
  232.3 5.3 fusion.77
  237.7 5.3 fusion.77
  243.1 5.3 fusion.77
  248.4 5.3 fusion.77
  256.6 130.4 %all-reduce.3.cloned.1.call-done = f32[1,512,512]{1,2,0:T(8,128)} async-done(((f32[1,512,512]{1,2,0:T(8,128)}), f32[1,512,512]{1,2,0:T(8,128)}) %all-reduce.3.cloned.1.call-update) | async-done | bytes 1048592 | tf_op jit(solution)/shard_map/psum | solution.py:49
  390.0 11.7 %custom-call.34 = f32[1,128,128]{2,1,0:T(8,128)S(1)} custom-call(f32[1,128,128]{2,1,0:T(8,128)S(1)} %cholesky.267), custom_call_target="Cholesky" | custom-call | tf_op jit(solution)/shard_map/jit(cholesky)/cholesky | solution.py:50
  401.7 9.8 %custom-call.35 = f32[1,1,128,128]{2,3,1,0:T(8,128)S(1)} custom-call(f32[1,1,128,128]{3,2,1,0:T(8,128)S(1)} %get-tuple-element.169), custom_call_target="InvertDiagBlocksLowerTriangular" | custom-call | tf_op jit(solution)/shard_map/jit(cholesky)/cholesky | solution.py:50
  412.4 11.7 %custom-call.36 = f32[1,128,128]{2,1,0:T(8,128)S(1)} custom-call(f32[1,128,128]{2,1,0:T(8,128)S(1)} %cholesky.271), custom_call_target="Cholesky" | custom-call | tf_op jit(solution)/shard_map/jit(cholesky)/cholesky | solution.py:50
  424.1 10.0 %custom-call.37 = f32[1,1,128,128]{2,3,1,0:T(8,128)S(1)} custom-call(f32[1,1,128,128]{3,2,1,0:T(8,128)S(1)} %get-tuple-element.166), custom_call_target="InvertDiagBlocksLowerTriangular" | custom-call | tf_op jit(solution)/shard_map/jit(cholesky)/cholesky | solution.py:50
  434.7 11.7 %custom-call.38 = f32[1,128,128]{2,1,0:T(8,128)S(1)} custom-call(f32[1,128,128]{2,1,0:T(8,128)S(1)} %cholesky.276), custom_call_target="Cholesky" | custom-call | tf_op jit(solution)/shard_map/jit(cholesky)/cholesky | solution.py:50
  447.2 9.8 %custom-call.39 = f32[1,1,128,128]{2,3,1,0:T(8,128)S(1)} custom-call(f32[1,1,128,128]{3,2,1,0:T(8,128)S(1)} %get-tuple-element.163), custom_call_target="InvertDiagBlocksLowerTriangular" | custom-call | tf_op jit(solution)/shard_map/jit(cholesky)/cholesky | solution.py:50
  457.6 11.7 %custom-call.40 = f32[1,128,128]{2,1,0:T(8,128)S(1)} custom-call(f32[1,128,128]{2,1,0:T(8,128)S(1)} %fusion.46), custom_call_target="Cholesky" | custom-call | tf_op jit(solution)/shard_map/jit(cholesky)/cholesky | solution.py:50
  473.6 8.1 %while.17 = (s32[]{:T(128)}, f32[1,512,512]{2,1,0:T(8,128)S(1)}, s32[4,2]{0,1:T(2,128)S(1)}, f32[4,1,128,128]{3,2,1,0:T(8,128)S(1)}, s32[]{:T(128)}) while((s32[]{:T(128)}, f32[1,512,512]{2,1,0:T(8,128)S(1)}, s32[4,2]{0,1:T(2,128)S(1)}, f32[4,1,128,128]{3,2,1,0:T(8,128)S(1)}, s32[]{:T(128)}) %tuple.68), condition=%wide.while_cond, body=%wide.while_body.sunk | while | flops 2 | bytes 131181 | solution.py:52
  481.7 39.3 %custom-call.41 = f32[1,4,128,128]{2,3,1,0:T(8,128)S(1)} custom-call(f32[1,4,128,128]{3,2,1,0:T(8,128)S(1)} %bitcast.228), custom_call_target="InvertDiagBlocksLowerTriangular" | custom-call | tf_op jit(solution)/shard_map/triangular_solve | solution.py:52
  525.0 27.2 %all-gather.2.cloned.1.call-done = bf16[1,2048,512]{1,2,0:T(8,128)(2,1)} async-done(((bf16[1,256,512]{1,2,0:T(8,128)(2,1)}), bf16[1,2048,512]{1,2,0:T(8,128)(2,1)}) %all-gather.2.cloned.1.call-update) | async-done | bytes 2097168 | tf_op jit(solution)/shard_map/all_gather | solution.py:57
  552.1 13.6 %fusion.31 = f32[512,1,3584]{2,0,1:T(8,128)} fusion(bf16[1,2048,3584]{2,1,0:T(8,128)(2,1)} %param.4, bf16[1,2048,512]{1,2,0:T(8,128)(2,1)} %all-gather.2.cloned.1.call-done), kind=kOutput, calls=%fused_computation.27 | convolution fusion | flops 7516192768 | bytes 24117248 | tf_op jit(solution)/shard_map/mdr,mdc->rmc/dot_general | solution.py:55
  565.7 127.9 %reduce-scatter.2.cloned.1.call-done = f32[128,1,3584]{2,0,1:T(8,128)} async-done(((f32[512,1,3584]{2,0,1:T(8,128)}), f32[128,1,3584]{2,0,1:T(8,128)}) %reduce-scatter.2.cloned.1.call-update) | async-done | bytes 1835024 | tf_op jit(solution)/shard_map/reduce_scatter | solution.py:61
  (70 shorter events, 53.2 us)
Async XLA Ops:
  29.6 167.7 %all-to-all-start = ((bf16[8,1,256,3584]{3,2,1,0:T(8,128)(2,1)}), bf16[8,1,256,3584]{3,2,1,0:T(8,128)(2,1)}, u32[]{:S(2)}, u32[]{:S(2)}) async-start(bf16[8,1,256,3584]{3,2,1,0:T(8,128)(2,1)} %bitcast_dynamic-update-slice_fusion.1), calls=%async_computation | async-start | bytes 29360128 | tf_op jit(solution)/shard_map/all_to_all | solution.py:28
  35.1 351.9 %all-reduce.3.cloned.1.call-start = ((), (), s32[]{:S(2)}) async-start(), calls=%async_computation.2 | async-start | bytes 2097152 | tf_op jit(solution)/shard_map/psum | solution.py:49
  255.8 296.3 %all-gather.2.cloned.1.call-start = ((), (), s32[]{:S(2)}) async-start(), calls=%async_computation.3 | async-start | bytes 2359296 | tf_op jit(solution)/shard_map/all_gather | solution.py:57
  524.9 168.7 %reduce-scatter.2.cloned.1.call-start = ((), (), s32[]{:S(2)}) async-start(), calls=%async_computation.4 | async-start | bytes 9175040 | tf_op jit(solution)/shard_map/reduce_scatter | solution.py:61
Sparse Core Ops, SparseCore 0:
  256.0 130.9 all-reduce.2
  525.0 27.0 all-gather.1
  565.8 127.7 reduce-scatter.1
